TPU v7x, 256 devices: a whole 4x4x8 slice. The times are simulated.
256 devices in a mesh: energy: 64 (over z, y, core), atoms: 4 (over x).
Axes of the slice: x: 4, y: 4, z: 8, core: 2. Of those that a mesh axis runs over, the one named last changes fastest.
Arguments:
- green: bfloat16 [1024, 256, 288], P('energy', 'atoms'), may hold values from -6 to 6
- superop: bfloat16 [4, 288, 288], replicated, may hold values from -0.1875 to 0.1875
- phonon: bfloat16 [64, 2048], replicated, may hold values from -0.1875 to 0.1875
- owner: int32 [256, 1], P('atoms'), may hold values from 0 to 63; in each aligned block of 64 rows (0 to 63, 64 to 127, ...) at most 4 rows name the same one
- neighbours: int32 [256, 4], P('atoms'), may hold values from -1 to 255, as said below
Outputs:
- self_energy: bfloat16 [1024, 256, 288], P('energy', 'atoms')
Inputs may be any that keep to these rules, and one draw needn't show every extreme that they name: `owner`: within each aligned block of 64 atoms (one atom group) no domain holds more than 4 atoms, and some domain holds exactly 4. `neighbours`: each entry is -1 or the index of an atom at most 8 away from the row's atom; some entry lies exactly 8 above its row's atom, in the next atom group.
All inputs are finite; a program needn't handle non-finite values.
Results may differ from a plain program's by a relative error of at most 0.0049.
Values may be sent and summed in bfloat16 or wider, within the bound.
No kernel may reach another device: no remote copies, remote signals or barrier semaphores. Data moves between devices by JAX's collectives and lax.ppermute only.
A program may use at most 64 MiB of HBM per device.

v0:
```python
import jax
import jax.numpy as jnp
from jax import lax
from jax.sharding import PartitionSpec as P

SPLIT = 2
HALO = 8
ATOMS_DEV = 1


def padded(block, sides, width):
    for axis, dim in sides:
        count = lax.axis_size(axis)
        forward = [(i, i + 1) for i in range(count - 1)]
        backward = [(target, source) for source, target in forward]
        low = lax.ppermute(
            lax.slice_in_dim(block, block.shape[dim] - width, None, axis=dim), axis, forward
        )
        high = lax.ppermute(lax.slice_in_dim(block, 0, width, axis=dim), axis, backward)
        block = jnp.concatenate([low, block, high], axis=dim)
    return block


def toeplitz_rows(kernel_row, count):
    length = 2 * count
    flipped = kernel_row[::-1]
    tiled = jnp.tile(flipped, count)[: count * (length - 1)]
    return tiled.reshape(count, length - 1)[:, count - 1 : 2 * count - 1]


def per_device(green, superop, phonon, owner, neighbours):
    local_energies = green.shape[0]
    group_size = green.shape[1]
    comps = green.shape[2]
    slots = neighbours.shape[1]
    half_width = comps // SPLIT
    group = lax.axis_index("atoms")
    widened = padded(green, (("atoms", 1),), HALO)
    present = neighbours >= 0
    target_rows = jnp.where(present, neighbours - group * group_size + HALO, 0)
    picked = jnp.take(widened, target_rows.reshape(-1), axis=1)
    picked = jnp.where(present.reshape(1, -1, 1), picked, jnp.zeros_like(picked))
    coupled = jnp.dot(
        picked.reshape(local_energies * group_size, slots * comps),
        superop.reshape(slots * comps, comps),
        preferred_element_type=jnp.float32,
    )
    coupled = coupled.reshape(local_energies, group_size, comps).astype(jnp.bfloat16)
    count = local_energies * lax.axis_size("energy")
    energy_rank = lax.axis_index("energy")
    first_atom = energy_rank * ATOMS_DEV
    mine = lax.dynamic_slice_in_dim(owner[:, 0], first_atom, ATOMS_DEV)

    def build_kernel(domain):
        return toeplitz_rows(phonon[domain], count)

    kernels = jax.vmap(build_kernel)(mine)
    split_blocks = coupled.reshape(local_energies, group_size, SPLIT, half_width)
    product = jnp.einsum(
        "oph,hoiw->poiw",
        kernels,
        lax.all_to_all(split_blocks, "energy", split_axis=1, concat_axis=0, tiled=True),
        preferred_element_type=jnp.float32,
    )
    result = lax.all_to_all(
        product.astype(jnp.bfloat16), "energy", split_axis=0, concat_axis=1, tiled=True
    )
    result = result.reshape(local_energies, group_size, comps)
    return result


def solution(mesh):
    return jax.shard_map(
        per_device,
        mesh=mesh,
        in_specs=(P("energy", "atoms", None), P(), P(), P("atoms", None), P("atoms", None)),
        out_specs=P("energy", "atoms", None),
        check_vma=False,
    )
```

profile of v0, /device:TPU:6, one launch (start us, length us, event | category | flops | bytes accessed | tf_op | source)
XLA Modules:
  0.0 215.0 jit_solution(9396868010489294610)
XLA Ops:
  0.0 1.7 copy.36
  1.7 1.3 collective-permute-start
  3.0 4.6 %collective-permute-start.1 = (bf16[16,8,288]{2,0,1:T(8,128)(2,1)S(1)}, bf16[16,8,288]{2,0,1:T(8,128)(2,1)S(1)}, u32[]{:S(2)}, u32[]{:S(2)}) collective-permute-start(bf16[16,8,288]{2,0,1:T(8,128)(2,1)S(1)} %get-tuple-element.19), channel_id=1, source_target_pairs={{1,0},{2,1},{3,2},{5,4},{6,5},{7,6},{9,8},{10,9},{11,10},{13,12},{... | collective-permute-start | bytes 221192 | tf_op jit(solution)/shard_map/ppermute | solution.py:19
  7.6 1.2 constant_dynamic-slice_fusion.1
  10.8 0.8 constant_dynamic-slice_fusion
  11.5 1.5 reverse
  13.0 0.5 broadcast_bitcast_fusion
  13.6 24.7 %copy.51 = bf16[1,1,1024,2048]{3,1,2,0:T(2,128)(2,1)} copy(bf16[1,1,1024,2048]{3,2,1,0:T(8,128)(2,1)S(1)} %broadcast_bitcast_fusion) | data formatting | bytes 8388608
  39.2 0.2 pad_maximum_fusion
  39.4 2.8 %gather_fusion = bf16[256,16,288]{2,1,0:T(8,128)(2,1)} fusion(bf16[16,80,288]{2,0,1:T(8,128)(2,1)S(1)} %pad_maximum_fusion, s32[1024]{0:T(1024)S(1)} %pad_clamp_fusion), kind=kCustom, calls=%fused_computation | custom fusion | bytes 4719616 | tf_op jit(solution)/shard_map/jit(_take)/gather | solution.py:41
  42.2 3.2 %select_bitcast_fusion = bf16[16,256,288]{2,0,1:T(8,128)(2,1)S(1)} fusion(bf16[256,16,288]{2,1,0:T(8,128)(2,1)} %gather_fusion, pred[256,288]{1,0:T(8,128)(4,1)S(1)} %broadcast_in_dim.35, pred[256,288]{1,0:T(8,128)(4,1)S(1)} %broadcast_in_dim.38), kind=kLoop, calls=%fused_computation.2 | loop fusion | flops 2359296 | bytes 4866048 | tf_op jit(solution)/shard_map/jit(_where)/select_n | solution.py:42
  45.4 2.5 %copy.40 = bf16[16,256,288]{2,1,0:T(8,128)(2,1)} copy(bf16[16,256,288]{2,0,1:T(8,128)(2,1)S(1)} %select_bitcast_fusion) | data formatting | bytes 4718592 | tf_op jit(solution)/shard_map/jit(_where)/select_n | solution.py:42
  47.9 5.8 %select_n.60 = bf16[16,64,1152]{2,1,0:T(8,128)(2,1)S(1)} reshape(bf16[16,256,288]{2,1,0:T(8,128)(2,1)} %copy.40) | data formatting | bytes 4718592 | tf_op jit(solution)/shard_map/jit(_where)/select_n | solution.py:42
  53.7 2.3 %convolution_convert_fusion = bf16[16,64,288]{2,1,0:T(8,128)(2,1)} fusion(bf16[16,64,1152]{2,1,0:T(8,128)(2,1)S(1)} %select_n.60, bf16[1152,288,1]{1,0,2:T(8,128)(2,1)S(1)} %bitcast.36), kind=kOutput, calls=%fused_computation.6 | convolution fusion | flops 679772160 | bytes 3612672 | tf_op jit(solution)/shard_map/dot_general | solution.py:43
  56.0 3.1 %reshape.127 = bf16[16,64,2,144]{3,2,1,0:T(2,128)(2,1)S(1)} reshape(bf16[16,64,288]{2,1,0:T(8,128)(2,1)} %convolution_convert_fusion) | data formatting | bytes 1179648 | tf_op jit(solution)/shard_map/reshape | solution.py:58
  59.2 2.2 %copy.42 = bf16[16,64,2,144]{3,0,2,1:T(8,128)(2,1)} copy(bf16[16,64,2,144]{3,2,1,0:T(2,128)(2,1)S(1)} %reshape.127) | data formatting | bytes 1179648 | tf_op jit(solution)/shard_map/reshape | solution.py:58
  61.4 12.3 %all-to-all-start = ((bf16[16,64,2,144]{3,0,2,1:T(8,128)(2,1)}), bf16[16,64,2,144]{3,0,2,1:T(8,128)(2,1)S(1)}, u32[]{:S(2)}, u32[]{:S(2)}) async-start(bf16[16,64,2,144]{3,0,2,1:T(8,128)(2,1)} %copy.42), calls=%async_computation | async-start | bytes 2097152 | tf_op jit(solution)/shard_map/all_to_all | solution.py:62
  73.7 84.7 %slice_reduce_fusion = bf16[2096128]{0:T(1024)(128)(2,1)} fusion(bf16[1,2097152]{1,0:T(2,128)(2,1)} %bitcast.37), kind=kLoop, calls=%fused_computation.1 | loop fusion | bytes 8384512 | tf_op jit(solution)/shard_map/vmap()/slice | solution.py:27
  158.4 10.7 %reshape.129 = bf16[1,1024,2047]{2,1,0:T(8,128)(2,1)} reshape(bf16[2096128]{0:T(1024)(128)(2,1)} %slice_reduce_fusion) | data formatting | bytes 8384512 | tf_op jit(solution)/shard_map/vmap()/reshape | solution.py:28
  169.1 3.6 %fusion.2 = bf16[1024,1,2,144]{0,3,2,1:T(8,128)(2,1)S(1)} fusion(bf16[1024,2,144]{2,0,1:T(8,128)(2,1)S(1)} %bitcast.40, bf16[1,1024,2047]{2,1,0:T(8,128)(2,1)} %reshape.129), kind=kOutput, calls=%fused_computation.8 | convolution fusion | flops 604274688 | bytes 3276800 | tf_op jit(solution)/shard_map/oph,hoiw->poiw/dot_general | solution.py:59
  172.7 0.9 copy.45
  173.6 38.8 %all_to_all.30 = bf16[1024,1,2,144]{3,2,1,0:T(2,128)(2,1)S(1)} all-to-all(bf16[1024,1,2,144]{3,2,1,0:T(2,128)(2,1)S(1)} %copy.45), channel_id=1, replica_groups=mesh['energy'=64,'atoms'=4] {'energy'}, dimensions={0} | all-to-all | bytes 1179648 | tf_op jit(solution)/shard_map/all_to_all | solution.py:65
  212.5 1.1 copy.47
  213.6 1.4 reshape.131
  (22 shorter events, 1.2 us)
Async XLA Ops:
  0.0 53.7 %copy-start = (bf16[4,288,288]{2,1,0:T(8,128)(2,1)S(1)}, bf16[4,288,288]{2,1,0:T(8,128)(2,1)}, u32[]{:S(2)}) copy-start(bf16[4,288,288]{2,1,0:T(8,128)(2,1)} %param.6) | copy-start | bytes 1990660
  1.7 37.5 %collective-permute-start = (bf16[16,8,288]{2,0,1:T(8,128)(2,1)S(1)}, bf16[16,8,288]{2,0,1:T(8,128)(2,1)S(1)}, u32[]{:S(2)}, u32[]{:S(2)}) collective-permute-start(bf16[16,8,288]{2,0,1:T(8,128)(2,1)S(1)} %get-tuple-element.18), channel_id=1, source_target_pairs={{0,1},{1,2},{2,3},{4,5},{5,6},{6,7},{8,9},{9,10},{10,11},{12,13},{... | collective-permute-start | bytes 221192 | tf_op jit(solution)/shard_map/ppermute | solution.py:16
  3.0 36.2 %collective-permute-start.1 = (bf16[16,8,288]{2,0,1:T(8,128)(2,1)S(1)}, bf16[16,8,288]{2,0,1:T(8,128)(2,1)S(1)}, u32[]{:S(2)}, u32[]{:S(2)}) collective-permute-start(bf16[16,8,288]{2,0,1:T(8,128)(2,1)S(1)} %get-tuple-element.19), channel_id=1, source_target_pairs={{1,0},{2,1},{3,2},{5,4},{6,5},{7,6},{9,8},{10,9},{11,10},{13,12},{... | collective-permute-start | bytes 221192 | tf_op jit(solution)/shard_map/ppermute | solution.py:19
  13.5 24.7 %copy-start.1 = (s32[64,4]{0,1:T(4,128)S(1)}, s32[64,4]{0,1:T(4,128)}, u32[]{:S(2)}) copy-start(s32[64,4]{0,1:T(4,128)} %param.9) | copy-start | bytes 3076
  61.4 107.6 %all-to-all-start = ((bf16[16,64,2,144]{3,0,2,1:T(8,128)(2,1)}), bf16[16,64,2,144]{3,0,2,1:T(8,128)(2,1)S(1)}, u32[]{:S(2)}, u32[]{:S(2)}) async-start(bf16[16,64,2,144]{3,0,2,1:T(8,128)(2,1)} %copy.42), calls=%async_computation | async-start | bytes 2097152 | tf_op jit(solution)/shard_map/all_to_all | solution.py:62
where the time goes:
time: 216 us; the launch traced here: 215 us
  local copies, waits for them, and re-layouts  147 us (68%)
  blocking collectives  38.8 us (18%)
  starting transfers between devices  18.1 us (8%)
  matrix products  5.92 us (3%)
  other arithmetic  3.44 us (2%)
    slice x1, local copies, waits for them, and re-layouts, toeplitz_rows(): tiled = jnp.tile(flipped, count)[:count * (length - 1)]  84.7 us
    all_to_all x1, blocking collectives, per_device(): lax.all_to_all(product.astype(jnp.bfloat16), 'energy', split_axis=0, conc...  38.8 us
    unnamed x8, local copies, waits for them, and re-layouts  28.3 us
    all_to_all x1, starting transfers between devices, per_device(): lax.all_to_all(split_blocks, 'energy', split_axis=1, concat_axis=0, tiled...  12.3 us
    reshape x1, local copies, waits for them, and re-layouts, toeplitz_rows(): return tiled.reshape(count, length - 1)[:, count - 1:2 * count - 1]  10.7 us
    select_n x2, local copies, waits for them, and re-layouts, per_device(): jnp.where(present.reshape(1, -1, 1), picked, jnp.zeros_like(picked))  8.28 us
    reshape x2, local copies, waits for them, and re-layouts, per_device(): coupled.reshape(local_energies, group_size, SPLIT, half_width)  5.32 us
    ppermute x1, starting transfers between devices, padded(): lax.ppermute(lax.slice_in_dim(block, 0, width, axis=dim), axis, backward)  4.55 us
  transfers between devices with their start and end apart: 3, of which 0 were waited for; matrix products, arithmetic and copies ran while one was open for 58% of the time, Pallas kernels for 0%

commit v1 on v0

--- a/solution.py
+++ b/solution.py
@@ -62,8 +62,14 @@
         lax.all_to_all(split_blocks, "energy", split_axis=1, concat_axis=0, tiled=True),
         preferred_element_type=jnp.float32,
     )
-    result = lax.all_to_all(
-        product.astype(jnp.bfloat16), "energy", split_axis=0, concat_axis=1, tiled=True
+    result = jnp.concatenate(
+        lax.all_to_all(
+            jnp.stack(jnp.split(product.astype(jnp.bfloat16), lax.axis_size("energy"), axis=0)),
+            "energy",
+            0,
+            0,
+        ),
+        axis=1,
     )
     result = result.reshape(local_energies, group_size, comps)
     return result

time: 216 us -> 319 us (1.48); the launches traced: 215 us -> 314 us
  local copies, waits for them, and re-layouts: 147 us -> 245 us
    another operation x0 -> x70, local copies, waits for them, and re-layouts: none -> 72.5 us  [the longest x69 71.1 us: per_device(): jnp.stack(jnp.split(product.astype(jnp.bfloat16), lax.axis_size('energy')...]
    unnamed x8 -> x77, local copies, waits for them, and re-layouts: 28.3 us -> 57.2 us
  transfers between devices with their start and end apart: 3 -> 3, of which waited for: 0 -> 0; matrix products, arithmetic and copies ran while one was open for 58% -> 40% of each run, Pallas kernels for 0% -> 0%
where the time goes in v1:
time: 319 us; the launch traced here: 314 us
  local copies, waits for them, and re-layouts  245 us (77%)
  blocking collectives  38.8 us (12%)
  starting transfers between devices  18.1 us (6%)
  matrix products  5.92 us (2%)
  other arithmetic  3.44 us (1%)
    slice x1, local copies, waits for them, and re-layouts, toeplitz_rows(): tiled = jnp.tile(flipped, count)[:count * (length - 1)]  84.7 us
    another operation x69, local copies, waits for them, and re-layouts, per_device(): jnp.stack(jnp.split(product.astype(jnp.bfloat16), lax.axis_size('energy')...  71.1 us
    unnamed x77, local copies, waits for them, and re-layouts  57.2 us
    all_to_all x1, blocking collectives, per_device(): lax.all_to_all(jnp.stack(jnp.split(product.astype(jnp.bfloat16), lax.axis...  38.8 us
    all_to_all x1, starting transfers between devices, per_device(): lax.all_to_all(split_blocks, 'energy', split_axis=1, concat_axis=0, tiled...  12.3 us
    reshape x1, local copies, waits for them, and re-layouts, toeplitz_rows(): return tiled.reshape(count, length - 1)[:, count - 1:2 * count - 1]  10.7 us
    select_n x2, local copies, waits for them, and re-layouts, per_device(): jnp.where(present.reshape(1, -1, 1), picked, jnp.zeros_like(picked))  8.25 us
  transfers between devices with their start and end apart: 3, of which 0 were waited for; matrix products, arithmetic and copies ran while one was open for 40% of the time, Pallas kernels for 0%

profile of v1, /device:TPU:6, one launch (start us, length us, event | category | flops | bytes accessed | tf_op | source)
XLA Modules:
  0.0 314.1 jit_solution(2096782755567653543)
XLA Ops:
  0.0 1.7 copy.99
  3.0 4.6 %collective-permute-start.1 = (bf16[16,8,288]{2,0,1:T(8,128)(2,1)S(1)}, bf16[16,8,288]{2,0,1:T(8,128)(2,1)S(1)}, u32[]{:S(2)}, u32[]{:S(2)}) collective-permute-start(bf16[16,8,288]{2,0,1:T(8,128)(2,1)S(1)} %get-tuple-element.19), channel_id=1, source_target_pairs={{1,0},{2,1},{3,2},{5,4},{6,5},{7,6},{9,8},{10,9},{11,10},{13,12},{... | collective-permute-start | bytes 221192 | tf_op jit(solution)/shard_map/ppermute | solution.py:19
  13.6 24.7 %copy.176 = bf16[1,1,1024,2048]{3,1,2,0:T(2,128)(2,1)} copy(bf16[1,1,1024,2048]{3,2,1,0:T(8,128)(2,1)S(1)} %broadcast_bitcast_fusion) | data formatting | bytes 8388608
  39.4 2.8 gather_fusion
  42.2 3.2 %select_bitcast_fusion = bf16[16,256,288]{2,0,1:T(8,128)(2,1)S(1)} fusion(bf16[256,16,288]{2,1,0:T(8,128)(2,1)} %gather_fusion, pred[256,288]{1,0:T(8,128)(4,1)S(1)} %broadcast_in_dim.35, pred[256,288]{1,0:T(8,128)(4,1)S(1)} %broadcast_in_dim.38), kind=kLoop, calls=%fused_computation.2 | loop fusion | flops 2359296 | bytes 4866048 | tf_op jit(solution)/shard_map/jit(_where)/select_n | solution.py:42
  45.4 2.4 copy.103
  47.9 5.8 %select_n.60 = bf16[16,64,1152]{2,1,0:T(8,128)(2,1)S(1)} reshape(bf16[16,256,288]{2,1,0:T(8,128)(2,1)} %copy.103) | data formatting | bytes 4718592 | tf_op jit(solution)/shard_map/jit(_where)/select_n | solution.py:42
  53.7 2.3 convolution_convert_fusion
  56.0 3.1 %reshape.126 = bf16[16,64,2,144]{3,2,1,0:T(2,128)(2,1)S(1)} reshape(bf16[16,64,288]{2,1,0:T(8,128)(2,1)} %convolution_convert_fusion) | data formatting | bytes 1179648 | tf_op jit(solution)/shard_map/reshape | solution.py:58
  59.1 2.2 copy.105
  61.3 12.3 %all-to-all-start = ((bf16[16,64,2,144]{3,0,2,1:T(8,128)(2,1)}), bf16[16,64,2,144]{3,0,2,1:T(8,128)(2,1)S(1)}, u32[]{:S(2)}, u32[]{:S(2)}) async-start(bf16[16,64,2,144]{3,0,2,1:T(8,128)(2,1)} %copy.105), calls=%async_computation | async-start | bytes 2097152 | tf_op jit(solution)/shard_map/all_to_all | solution.py:62
  73.6 84.7 %slice_reduce_fusion = bf16[2096128]{0:T(1024)(128)(2,1)} fusion(bf16[1,2097152]{1,0:T(2,128)(2,1)} %bitcast.163), kind=kLoop, calls=%fused_computation.1 | loop fusion | bytes 8384512 | tf_op jit(solution)/shard_map/vmap()/slice | solution.py:27
  158.3 10.7 %reshape.128 = bf16[1,1024,2047]{2,1,0:T(8,128)(2,1)} reshape(bf16[2096128]{0:T(1024)(128)(2,1)} %slice_reduce_fusion) | data formatting | bytes 8384512 | tf_op jit(solution)/shard_map/vmap()/reshape | solution.py:28
  169.1 3.6 %fusion.2 = bf16[1024,1,2,144]{0,3,2,1:T(8,128)(2,1)S(1)} fusion(bf16[1024,2,144]{2,0,1:T(8,128)(2,1)S(1)} %bitcast.166, bf16[1,1024,2047]{2,1,0:T(8,128)(2,1)} %reshape.128), kind=kOutput, calls=%fused_computation.8 | convolution fusion | flops 604274688 | bytes 3276800 | tf_op jit(solution)/shard_map/oph,hoiw->poiw/dot_general | solution.py:59
  187.6 1.6 copy.115
  190.7 1.6 copy.117
  192.2 1.6 copy.118
  203.1 1.6 copy.125
  214.0 1.6 copy.132
  220.3 1.6 copy.136
  223.4 1.6 copy.138
  228.1 1.6 copy.141
  240.5 1.6 copy.149
  272.9 38.8 %all_to_all.20 = bf16[64,16,1,2,144]{4,1,3,2,0:T(8,128)(2,1)S(1)} all-to-all(bf16[64,16,1,2,144]{4,1,3,2,0:T(8,128)(2,1)S(1)} %constant_dynamic-update-slice_fusion), channel_id=1, replica_groups=mesh['energy'=64,'atoms'=4] {'energy'}, dimensions={0} | all-to-all | bytes 1179648 | tf_op jit(solution)/shard_map/all_to_all | solution.py:66
  (158 shorter events, 94.9 us)
Async XLA Ops:
  0.0 53.7 %copy-start = (bf16[4,288,288]{2,1,0:T(8,128)(2,1)S(1)}, bf16[4,288,288]{2,1,0:T(8,128)(2,1)}, u32[]{:S(2)}) copy-start(bf16[4,288,288]{2,1,0:T(8,128)(2,1)} %param.6) | copy-start | bytes 1990660
  1.7 37.5 %collective-permute-start = (bf16[16,8,288]{2,0,1:T(8,128)(2,1)S(1)}, bf16[16,8,288]{2,0,1:T(8,128)(2,1)S(1)}, u32[]{:S(2)}, u32[]{:S(2)}) collective-permute-start(bf16[16,8,288]{2,0,1:T(8,128)(2,1)S(1)} %get-tuple-element.18), channel_id=1, source_target_pairs={{0,1},{1,2},{2,3},{4,5},{5,6},{6,7},{8,9},{9,10},{10,11},{12,13},{... | collective-permute-start | bytes 221192 | tf_op jit(solution)/shard_map/ppermute | solution.py:16
  3.0 36.2 %collective-permute-start.1 = (bf16[16,8,288]{2,0,1:T(8,128)(2,1)S(1)}, bf16[16,8,288]{2,0,1:T(8,128)(2,1)S(1)}, u32[]{:S(2)}, u32[]{:S(2)}) collective-permute-start(bf16[16,8,288]{2,0,1:T(8,128)(2,1)S(1)} %get-tuple-element.19), channel_id=1, source_target_pairs={{1,0},{2,1},{3,2},{5,4},{6,5},{7,6},{9,8},{10,9},{11,10},{13,12},{... | collective-permute-start | bytes 221192 | tf_op jit(solution)/shard_map/ppermute | solution.py:19
  13.5 24.7 %copy-start.4 = (s32[64,4]{0,1:T(4,128)S(1)}, s32[64,4]{0,1:T(4,128)}, u32[]{:S(2)}) copy-start(s32[64,4]{0,1:T(4,128)} %param.9) | copy-start | bytes 3076
  61.3 107.7 %all-to-all-start = ((bf16[16,64,2,144]{3,0,2,1:T(8,128)(2,1)}), bf16[16,64,2,144]{3,0,2,1:T(8,128)(2,1)S(1)}, u32[]{:S(2)}, u32[]{:S(2)}) async-start(bf16[16,64,2,144]{3,0,2,1:T(8,128)(2,1)} %copy.105), calls=%async_computation | async-start | bytes 2097152 | tf_op jit(solution)/shard_map/all_to_all | solution.py:62
  242.8 29.8 %copy-start.3 = (bf16[1,16,1,2,144]{4,1,3,2,0:T(8,128)(2,1)S(1)}, bf16[1,16,1,2,144]{4,1,3,2,0:T(8,128)(2,1)}, u32[]{:S(2)}) copy-start(bf16[1,16,1,2,144]{4,1,3,2,0:T(8,128)(2,1)} %copy.148) | copy-start | bytes 27652
  242.8 29.8 %copy-start.2 = (bf16[1,16,1,2,144]{4,1,3,2,0:T(8,128)(2,1)S(1)}, bf16[1,16,1,2,144]{4,1,3,2,0:T(8,128)(2,1)}, u32[]{:S(2)}) copy-start(bf16[1,16,1,2,144]{4,1,3,2,0:T(8,128)(2,1)} %copy.149) | copy-start | bytes 27652
  242.8 29.8 %copy-start.1 = (bf16[1,16,1,2,144]{4,1,3,2,0:T(8,128)(2,1)S(1)}, bf16[1,16,1,2,144]{4,1,3,2,0:T(8,128)(2,1)}, u32[]{:S(2)}) copy-start(bf16[1,16,1,2,144]{4,1,3,2,0:T(8,128)(2,1)} %copy.150) | copy-start | bytes 27652
